TPU v7x, 128 devices: a whole 4x4x4 slice. The times are simulated.
128 devices in a mesh: blk: 8 (over z, x_lo), rep: 16 (over x_hi, y, core).
Axes of the slice: x: 4 (x_hi: 2, x_lo: 2; x = x_hi * 2 + x_lo), y: 4, z: 4, core: 2. Of those that a mesh axis runs over, the one named last changes fastest.
Arguments:
- raw_features: bfloat16 [131072, 512], P(('blk', 'rep')), may hold values from -6 to 6
- move_plan: int32 [8, 16, 16], P('blk'), may hold values from 8 to 64, as said below
- weight: bfloat16 [512, 512], replicated, may hold values from -0.25 to 0.25
- bias_vector: float32 [512], replicated, may hold values from -3 to 3
- tile_rows: int32 [8, 16, 16, 6], P('blk', 'rep'), may hold values from 0 to 31, as said below
- tile_values: bfloat16 [8, 16, 16, 6, 256, 256], P('blk', 'rep'), may hold values from -0.0546875 to 0.0546875
- grad_out: bfloat16 [65536, 512], P(('blk', 'rep')), may hold values from -6 to 6
Outputs:
- projected: bfloat16 [65536, 512], P(('blk', 'rep'))
- activated: bfloat16 [65536, 512], P(('blk', 'rep'))
- feature_grad: bfloat16 [65536, 512], P(('blk', 'rep'))
- weight_grad: float32 [512, 512], replicated
- bias_grad: float32 [512], replicated
Inputs may be any that keep to these rules, and one draw needn't show every extreme that they name: For every partition p and destination e the counts move_plan[p, s, e] over sources s sum to 512; the counts of one source over destinations sum to at most 1024, and some source of every partition sends 64 rows to every destination. `tile_rows`: the 6 row tiles listed for one column tile of a device are distinct.
All inputs are finite; a program needn't handle non-finite values.
Results may differ from a plain program's by a relative error of at most 0.018.
Values may be sent and summed in bfloat16 or wider, within the bound.
No kernel may reach another device: no remote copies, remote signals or barrier semaphores. Data moves between devices by JAX's collectives and lax.ppermute only.
A program may use at most 192 MiB of HBM per device.

v0:
```python
import math
import jax
import jax.numpy as jnp
from jax import lax
from jax.sharding import PartitionSpec as P


def silu_slope(values):
    sigma = jax.nn.sigmoid(values)
    return sigma * (1.0 + values * (1.0 - sigma))


def per_device(raw_features, move_plan, weight, bias_vector, tile_rows, tile_values, grad_out):
    rep_size = lax.axis_size("rep")
    own_index = lax.axis_index("rep")
    dev_rows, feature_width = grad_out.shape
    raw_rows = raw_features.shape[0]
    capacity = 4 * (dev_rows // (2 * rep_size))
    counts = move_plan[0]
    tile_stack = tile_values[0, 0]
    row_lists = tile_rows[0, 0]
    tile_size = tile_stack.shape[2]
    row_tiles = rep_size * dev_rows // tile_size
    root_count = math.sqrt(dev_rows * lax.axis_size("blk") * rep_size)
    sent_counts = lax.dynamic_index_in_dim(counts, own_index, 0, keepdims=False)
    first_rows = jnp.cumsum(sent_counts) - sent_counts
    slot_rows = first_rows[:, None] + jnp.arange(capacity, dtype=jnp.int32)[None, :]
    outgoing = raw_features[jnp.minimum(slot_rows, raw_rows - 1)]
    incoming = lax.all_to_all(outgoing, "rep", split_axis=0, concat_axis=0, tiled=True)
    recv_counts = lax.dynamic_index_in_dim(counts, own_index, 1, keepdims=False)
    inclusive = jnp.cumsum(recv_counts)
    exclusive = inclusive - recv_counts
    positions = jnp.arange(dev_rows, dtype=jnp.int32)
    sources = jnp.sum((inclusive[None, :] <= positions[:, None]).astype(jnp.int32), axis=1)
    selector = sources[:, None] == jnp.arange(rep_size, dtype=jnp.int32)[None, :]
    offsets = jnp.sum(jnp.where(selector, exclusive[None, :], 0), axis=1)
    features = incoming.reshape(rep_size * capacity, feature_width)[
        sources * capacity + positions - offsets
    ]
    projected = jnp.dot(features, weight, preferred_element_type=jnp.float32).astype(jnp.bfloat16)
    zero_rows = jnp.zeros((row_tiles, tile_size, feature_width), jnp.float32)
    shard_rows = lax.all_gather(projected, "blk", axis=0, tiled=True)

    def column_step(step_index, running):
        adjacency_tile = lax.dynamic_index_in_dim(tile_stack, step_index, 0, keepdims=False)
        targets = lax.dynamic_index_in_dim(row_lists, step_index, 0, keepdims=False)
        inputs = lax.dynamic_slice_in_dim(shard_rows, step_index * tile_size, tile_size, 0)
        matmul_result = jnp.einsum(
            "jab,bf->jaf", adjacency_tile, inputs, preferred_element_type=jnp.float32
        )
        return running.at[targets].add(matmul_result)

    partial_value = lax.fori_loop(0, shard_rows.shape[0] // tile_size, column_step, zero_rows)
    partial_value = partial_value.reshape(row_tiles * tile_size, feature_width)
    preact = (
        lax.psum_scatter(
            partial_value.astype(jnp.bfloat16), "rep", scatter_dimension=0, tiled=True
        ).astype(jnp.float32)
        + bias_vector
    )
    own_grad = (grad_out.astype(jnp.float32) * silu_slope(preact)).astype(jnp.bfloat16)
    pre_grad = lax.all_gather(own_grad, "rep", axis=0, tiled=True)
    activated = jax.nn.silu(preact).astype(jnp.bfloat16)
    grad_tiles = pre_grad.reshape(row_tiles, tile_size, feature_width)
    column_indices = lax.axis_size("blk") * dev_rows // tile_size
    adjacency_tile = tile_stack
    targets = row_lists
    selected_rows = grad_tiles[targets]
    column_contribution = jnp.einsum(
        "nzqm,nzqg->nmg", adjacency_tile, selected_rows, preferred_element_type=jnp.float32
    )
    proj_grad = lax.psum_scatter(
        column_contribution.reshape(column_indices * tile_size, feature_width).astype(jnp.bfloat16),
        "blk",
        scatter_dimension=0,
        tiled=True,
    )
    local_weight = jnp.einsum("nf,ng->fg", features, proj_grad, preferred_element_type=jnp.float32)
    local_bias = jnp.sum(own_grad.astype(jnp.float32), axis=0)
    weight_sum, bias_sum = lax.psum((local_weight, local_bias), ("blk", "rep"))
    feature_grad = jnp.einsum(
        "ng,fg->nf", proj_grad, weight, preferred_element_type=jnp.float32
    ).astype(jnp.bfloat16)
    return (projected, activated, feature_grad, weight_sum / root_count, bias_sum / root_count)


def solution(mesh):
    return jax.shard_map(
        per_device,
        mesh=mesh,
        in_specs=(
            P(("blk", "rep"), None),
            P("blk", None, None),
            P(),
            P(),
            P("blk", "rep", None, None),
            P("blk", "rep", None, None, None, None),
            P(("blk", "rep"), None),
        ),
        out_specs=(
            P(("blk", "rep"), None),
            P(("blk", "rep"), None),
            P(("blk", "rep"), None),
            P(),
            P(),
        ),
        check_vma=False,
    )
```

profile of v0, /device:TPU:1, one launch (start us, length us, event | category | flops | bytes accessed | tf_op | source)
XLA Modules:
  0.0 759.6 jit_solution(11965677881912372824)
XLA Ops:
  9.1 5.1 gather_fusion
  14.2 8.4 %all-to-all-start = ((bf16[16,64,512]{2,1,0:T(8,128)(2,1)}), bf16[16,64,512]{2,1,0:T(8,128)(2,1)S(1)}, u32[]{:S(2)}, u32[]{:S(2)}) async-start(bf16[16,64,512]{2,1,0:T(8,128)(2,1)} %bitcast.6), calls=%async_computation | async-start | bytes 2097152 | tf_op jit(solution)/shard_map/all_to_all | solution.py:29
  23.9 15.8 %all-to-all-done = bf16[16,64,512]{2,1,0:T(8,128)(2,1)S(1)} async-done(((bf16[16,64,512]{2,1,0:T(8,128)(2,1)}), bf16[16,64,512]{2,1,0:T(8,128)(2,1)S(1)}, u32[]{:S(2)}, u32[]{:S(2)}) %all-to-all-start) | async-done | bytes 1048608 | tf_op jit(solution)/shard_map/all_to_all | solution.py:29
  39.7 2.0 gather_fusion.1
  43.1 89.0 %all-gather.3.cloned.1.call-done = bf16[4096,512]{1,0:T(8,128)(2,1)} async-done(((bf16[512,512]{1,0:T(8,128)(2,1)}), bf16[4096,512]{1,0:T(8,128)(2,1)}) %all-gather.3.cloned.1.call-update) | async-done | bytes 4194320 | tf_op jit(solution)/shard_map/all_gather | solution.py:42
  132.1 7.9 %broadcast_in_dim.18 = f32[32,256,512]{2,1,0:T(8,128)} broadcast(f32[]{:T(128)} %constant.89.clone.1), dimensions={} | broadcast | bytes 16777220 | tf_op jit(solution)/shard_map/broadcast_in_dim | solution.py:41
  139.9 150.8 %while.13 = (s32[]{:T(128)}, f32[32,256,512]{2,1,0:T(8,128)}, s32[16,6]{1,0:T(8,128)S(1)}, bf16[16,6,256,256]{3,2,1,0:T(8,128)(2,1)}, bf16[4096,512]{1,0:T(8,128...) while((s32[]{:T(128)}, f32[32,256,512]{2,1,0:T(8,128)}, s32[16,6]{1,0:T(8,128)S(1)}, ...), condition=%wide.region_6.7_spmd, body=%wide.region_4.6_spmd.sunk | while | flops 403439648 | bytes 13632219 | solution.py:53
  139.9 1.8 fusion.25
  141.7 7.6 %scatter_fusion = f32[32,256,512]{2,1,0:T(8,128)} fusion(f32[32,256,512]{2,1,0:T(8,128)} %get-tuple-element.171, s32[6]{0:T(128)S(1)} %fusion.24, f32[6,256,512]{2,1,0:T(8,128)S(1)} %fusion.25), kind=kCustom, calls=%fused_computation.3.clone.1 | custom fusion | flops 786432 | bytes 9437208 | tf_op jit(solution)/shard_map/while/body/eval_jaxpr/scatter-add | solution.py:51
  149.3 1.7 fusion.25
  151.1 7.7 %scatter_fusion = f32[32,256,512]{2,1,0:T(8,128)} fusion(f32[32,256,512]{2,1,0:T(8,128)} %get-tuple-element.171, s32[6]{0:T(128)S(1)} %fusion.24, f32[6,256,512]{2,1,0:T(8,128)S(1)} %fusion.25), kind=kCustom, calls=%fused_computation.3.clone.1 | custom fusion | flops 786432 | bytes 9437208 | tf_op jit(solution)/shard_map/while/body/eval_jaxpr/scatter-add | solution.py:51
  158.8 1.7 fusion.25
  160.6 7.6 %scatter_fusion = f32[32,256,512]{2,1,0:T(8,128)} fusion(f32[32,256,512]{2,1,0:T(8,128)} %get-tuple-element.171, s32[6]{0:T(128)S(1)} %fusion.24, f32[6,256,512]{2,1,0:T(8,128)S(1)} %fusion.25), kind=kCustom, calls=%fused_computation.3.clone.1 | custom fusion | flops 786432 | bytes 9437208 | tf_op jit(solution)/shard_map/while/body/eval_jaxpr/scatter-add | solution.py:51
  170.0 7.7 %scatter_fusion = f32[32,256,512]{2,1,0:T(8,128)} fusion(f32[32,256,512]{2,1,0:T(8,128)} %get-tuple-element.171, s32[6]{0:T(128)S(1)} %fusion.24, f32[6,256,512]{2,1,0:T(8,128)S(1)} %fusion.25), kind=kCustom, calls=%fused_computation.3.clone.1 | custom fusion | flops 786432 | bytes 9437208 | tf_op jit(solution)/shard_map/while/body/eval_jaxpr/scatter-add | solution.py:51
  177.7 1.8 fusion.25
  179.5 7.7 %scatter_fusion = f32[32,256,512]{2,1,0:T(8,128)} fusion(f32[32,256,512]{2,1,0:T(8,128)} %get-tuple-element.171, s32[6]{0:T(128)S(1)} %fusion.24, f32[6,256,512]{2,1,0:T(8,128)S(1)} %fusion.25), kind=kCustom, calls=%fused_computation.3.clone.1 | custom fusion | flops 786432 | bytes 9437208 | tf_op jit(solution)/shard_map/while/body/eval_jaxpr/scatter-add | solution.py:51
  187.1 1.8 fusion.25
  188.9 7.6 scatter_fusion
  198.3 7.7 %scatter_fusion = f32[32,256,512]{2,1,0:T(8,128)} fusion(f32[32,256,512]{2,1,0:T(8,128)} %get-tuple-element.171, s32[6]{0:T(128)S(1)} %fusion.24, f32[6,256,512]{2,1,0:T(8,128)S(1)} %fusion.25), kind=kCustom, calls=%fused_computation.3.clone.1 | custom fusion | flops 786432 | bytes 9437208 | tf_op jit(solution)/shard_map/while/body/eval_jaxpr/scatter-add | solution.py:51
  206.0 1.7 fusion.25
  207.8 7.6 %scatter_fusion = f32[32,256,512]{2,1,0:T(8,128)} fusion(f32[32,256,512]{2,1,0:T(8,128)} %get-tuple-element.171, s32[6]{0:T(128)S(1)} %fusion.24, f32[6,256,512]{2,1,0:T(8,128)S(1)} %fusion.25), kind=kCustom, calls=%fused_computation.3.clone.1 | custom fusion | flops 786432 | bytes 9437208 | tf_op jit(solution)/shard_map/while/body/eval_jaxpr/scatter-add | solution.py:51
  215.4 1.7 fusion.25
  217.1 7.6 scatter_fusion
  224.7 1.7 fusion.25
  226.5 7.6 %scatter_fusion = f32[32,256,512]{2,1,0:T(8,128)} fusion(f32[32,256,512]{2,1,0:T(8,128)} %get-tuple-element.171, s32[6]{0:T(128)S(1)} %fusion.24, f32[6,256,512]{2,1,0:T(8,128)S(1)} %fusion.25), kind=kCustom, calls=%fused_computation.3.clone.1 | custom fusion | flops 786432 | bytes 9437208 | tf_op jit(solution)/shard_map/while/body/eval_jaxpr/scatter-add | solution.py:51
  234.1 1.8 fusion.25
  235.9 7.7 %scatter_fusion = f32[32,256,512]{2,1,0:T(8,128)} fusion(f32[32,256,512]{2,1,0:T(8,128)} %get-tuple-element.171, s32[6]{0:T(128)S(1)} %fusion.24, f32[6,256,512]{2,1,0:T(8,128)S(1)} %fusion.25), kind=kCustom, calls=%fused_computation.3.clone.1 | custom fusion | flops 786432 | bytes 9437208 | tf_op jit(solution)/shard_map/while/body/eval_jaxpr/scatter-add | solution.py:51
  245.4 7.6 %scatter_fusion = f32[32,256,512]{2,1,0:T(8,128)} fusion(f32[32,256,512]{2,1,0:T(8,128)} %get-tuple-element.171, s32[6]{0:T(128)S(1)} %fusion.24, f32[6,256,512]{2,1,0:T(8,128)S(1)} %fusion.25), kind=kCustom, calls=%fused_computation.3.clone.1 | custom fusion | flops 786432 | bytes 9437208 | tf_op jit(solution)/shard_map/while/body/eval_jaxpr/scatter-add | solution.py:51
  253.0 1.8 fusion.25
  254.8 7.7 %scatter_fusion = f32[32,256,512]{2,1,0:T(8,128)} fusion(f32[32,256,512]{2,1,0:T(8,128)} %get-tuple-element.171, s32[6]{0:T(128)S(1)} %fusion.24, f32[6,256,512]{2,1,0:T(8,128)S(1)} %fusion.25), kind=kCustom, calls=%fused_computation.3.clone.1 | custom fusion | flops 786432 | bytes 9437208 | tf_op jit(solution)/shard_map/while/body/eval_jaxpr/scatter-add | solution.py:51
  262.5 1.7 fusion.25
  264.3 7.6 %scatter_fusion = f32[32,256,512]{2,1,0:T(8,128)} fusion(f32[32,256,512]{2,1,0:T(8,128)} %get-tuple-element.171, s32[6]{0:T(128)S(1)} %fusion.24, f32[6,256,512]{2,1,0:T(8,128)S(1)} %fusion.25), kind=kCustom, calls=%fused_computation.3.clone.1 | custom fusion | flops 786432 | bytes 9437208 | tf_op jit(solution)/shard_map/while/body/eval_jaxpr/scatter-add | solution.py:51
  271.9 1.7 fusion.25
  273.7 7.6 %scatter_fusion = f32[32,256,512]{2,1,0:T(8,128)} fusion(f32[32,256,512]{2,1,0:T(8,128)} %get-tuple-element.171, s32[6]{0:T(128)S(1)} %fusion.24, f32[6,256,512]{2,1,0:T(8,128)S(1)} %fusion.25), kind=kCustom, calls=%fused_computation.3.clone.1 | custom fusion | flops 786432 | bytes 9437208 | tf_op jit(solution)/shard_map/while/body/eval_jaxpr/scatter-add | solution.py:51
  281.3 1.8 fusion.25
  283.1 7.6 %scatter_fusion = f32[32,256,512]{2,1,0:T(8,128)} fusion(f32[32,256,512]{2,1,0:T(8,128)} %get-tuple-element.171, s32[6]{0:T(128)S(1)} %fusion.24, f32[6,256,512]{2,1,0:T(8,128)S(1)} %fusion.25), kind=kCustom, calls=%fused_computation.3.clone.1 | custom fusion | flops 786432 | bytes 9437208 | tf_op jit(solution)/shard_map/while/body/eval_jaxpr/scatter-add | solution.py:51
  290.7 9.1 %convert_element_type.41 = bf16[32,256,512]{2,1,0:T(8,128)(2,1)} convert(f32[32,256,512]{2,1,0:T(8,128)} %get-tuple-element.99) | non-fusion elementwise | flops 4194304 | bytes 25165824 | tf_op jit(solution)/shard_map/convert_element_type | solution.py:57
  299.9 101.1 %reduce-scatter.3.cloned.1.call-done = bf16[512,512]{1,0:T(8,128)(2,1)} async-done(((bf16[8192,512]{1,0:T(8,128)(2,1)}), bf16[512,512]{1,0:T(8,128)(2,1)}) %reduce-scatter.3.cloned.1.call-update) | async-done | bytes 524304 | tf_op jit(solution)/shard_map/reduce_scatter | solution.py:56
  401.0 2.5 convert_reduce_fusion
  403.8 73.5 %all-gather.5.cloned.1.call-done = bf16[8192,512]{1,0:T(8,128)(2,1)} async-done(((bf16[512,512]{1,0:T(8,128)(2,1)}), bf16[8192,512]{1,0:T(8,128)(2,1)}) %all-gather.5.cloned.1.call-update) | async-done | bytes 8388624 | tf_op jit(solution)/shard_map/all_gather | solution.py:62
  477.3 13.6 %gather_fusion.2 = bf16[96,256,512]{2,1,0:T(8,128)(2,1)} fusion(bf16[32,256,512]{2,1,0:T(8,128)(2,1)} %bitcast.59, s32[1024]{0:T(1024)S(1)} %pad_clamp_fusion), kind=kCustom, calls=%fused_computation.2 | custom fusion | bytes 50332032 | tf_op jit(solution)/shard_map/gather | solution.py:68
  490.9 17.4 %bitcast_convert_fusion = bf16[16,512,256]{1,2,0:T(8,128)(2,1)} fusion(bf16[16,6,256,512]{3,2,1,0:T(8,128)(2,1)} %bitcast.62, bf16[1,1,16,6,256,256]{5,4,3,2,1,0:T(8,128)(2,1)} %bitcast.65), kind=kOutput, calls=%fused_computation.14 | convolution fusion | flops 6444548096 | bytes 41943040 | tf_op jit(solution)/shard_map/nzqm,nzqg->nmg/dot_general | solution.py:69
  508.4 88.7 %reduce-scatter.5.cloned.1.call-done = bf16[512,512]{1,0:T(8,128)(2,1)} async-done(((bf16[4096,512]{1,0:T(8,128)(2,1)}), bf16[512,512]{1,0:T(8,128)(2,1)}) %reduce-scatter.5.cloned.1.call-update) | async-done | bytes 524304 | tf_op jit(solution)/shard_map/reduce_scatter | solution.py:72
  597.1 2.5 fusion.10
  599.6 64.9 %psum.15 = f32[512]{0:T(512)S(1)} all-reduce(f32[512]{0:T(512)S(1)} %get-tuple-element.125), channel_id=1, replica_groups=mesh['blk'=8,'rep'=16] {'blk','rep'}, use_global_device_ids=true, to_apply=%region_11.12 | all-reduce | flops 512 | bytes 4096 | tf_op jit(solution)/shard_map/psum | solution.py:80
  665.0 2.3 convolution_convert_fusion
  667.4 83.4 %all-reduce.2.cloned.1.call-done = f32[512,512]{1,0:T(8,128)} async-done(((f32[512,512]{1,0:T(8,128)}), f32[512,512]{1,0:T(8,128)}) %all-reduce.2.cloned.1.call-update) | async-done | bytes 1048592 | tf_op jit(solution)/shard_map/psum | solution.py:80
  750.8 2.3 broadcast_multiply_fusion
  (71 shorter events, 11.0 us)
Async XLA Ops:
  7.2 1.9 copy-start
  7.2 34.5 %copy-start.4 = (bf16[512,512]{1,0:T(8,128)(2,1)S(1)}, bf16[512,512]{1,0:T(8,128)(2,1)}, u32[]{:S(2)}) copy-start(bf16[512,512]{1,0:T(8,128)(2,1)} %param.11) | copy-start | bytes 1572868
  7.2 35.8 %copy-start.7 = (s32[1,1,16,6]{2,1,3,0:T(1,128)S(1)}, s32[1,1,16,6]{2,1,3,0:T(1,128)}, u32[]{:S(2)}) copy-start(s32[1,1,16,6]{2,1,3,0:T(1,128)} %param.13) | copy-start | bytes 1156
  14.2 25.5 %all-to-all-start = ((bf16[16,64,512]{2,1,0:T(8,128)(2,1)}), bf16[16,64,512]{2,1,0:T(8,128)(2,1)S(1)}, u32[]{:S(2)}, u32[]{:S(2)}) async-start(bf16[16,64,512]{2,1,0:T(8,128)(2,1)} %bitcast.6), calls=%async_computation | async-start | bytes 2097152 | tf_op jit(solution)/shard_map/all_to_all | solution.py:29
  22.6 109.4 %all-gather.3.cloned.1.call-start = ((), (), s32[]{:S(2)}) async-start(), calls=%async_computation.3 | async-start | bytes 4718592 | tf_op jit(solution)/shard_map/all_gather | solution.py:42
  41.7 98.2 %copy-start.2 = (bf16[512,512]{1,0:T(8,128)(2,1)}, bf16[512,512]{1,0:T(8,128)(2,1)S(1)}, u32[]{:S(2)}) copy-start(bf16[512,512]{1,0:T(8,128)(2,1)S(1)} %gather_fusion.1) | copy-start | bytes 1572868
  43.0 358.1 %reduce-scatter.3.cloned.1.call-start = ((), (), s32[]{:S(2)}) async-start(), calls=%async_computation.4 | async-start | bytes 8912896 | tf_op jit(solution)/shard_map/reduce_scatter | solution.py:56
  290.7 110.3 %copy-start.6 = (bf16[512,512]{1,0:T(8,128)(2,1)S(1)}, bf16[512,512]{1,0:T(8,128)(2,1)}, u32[]{:S(2)}) copy-start(bf16[512,512]{1,0:T(8,128)(2,1)} %param.15) | copy-start | bytes 1572868
  290.7 110.3 %copy-start.8 = (f32[512]{0:T(512)S(1)}, f32[512]{0:T(512)}, u32[]{:S(2)}) copy-start(f32[512]{0:T(512)} %param.12) | copy-start | bytes 6148
  299.9 177.4 %all-gather.5.cloned.1.call-start = ((), (), s32[]{:S(2)}) async-start(), calls=%async_computation.5 | async-start | bytes 8912896 | tf_op jit(solution)/shard_map/all_gather | solution.py:62
  403.6 193.5 %reduce-scatter.5.cloned.1.call-start = ((), (), s32[]{:S(2)}) async-start(), calls=%async_computation.6 | async-start | bytes 4718592 | tf_op jit(solution)/shard_map/reduce_scatter | solution.py:72
  490.9 106.2 %copy-start.3 = (bf16[512,512]{1,0:T(8,128)(2,1)S(1)}, bf16[512,512]{1,0:T(8,128)(2,1)}, u32[]{:S(2)}) copy-start(bf16[512,512]{1,0:T(8,128)(2,1)} %copy-done.2) | copy-start | bytes 1572868
  490.9 174.1 %copy-start.5 = (bf16[512,512]{1,0:T(8,128)(2,1)S(1)}, bf16[512,512]{1,0:T(8,128)(2,1)}, u32[]{:S(2)}) copy-start(bf16[512,512]{1,0:T(8,128)(2,1)} %param.11) | copy-start | bytes 1572868
  490.9 262.1 %copy-start.1 = (bf16[1024,512]{1,0:T(8,128)(2,1)S(1)}, bf16[1024,512]{1,0:T(8,128)(2,1)}, u32[]{:S(2)}) copy-start(bf16[1024,512]{1,0:T(8,128)(2,1)} %param.9) | copy-start | bytes 3145732
  508.3 242.5 %all-reduce.2.cloned.1.call-start = ((), (), s32[]{:S(2)}) async-start(), calls=%async_computation.7 | async-start | bytes 2097152 | tf_op jit(solution)/shard_map/psum | solution.py:80
Sparse Core Ops, SparseCore 0:
  43.1 88.9 all-gather.2
  300.0 100.9 reduce-scatter.2
  404.1 73.2 all-gather.4
  508.4 88.5 reduce-scatter.4
  602.3 148.4 all-reduce.1
where the time goes:
time: 762 us; the launch traced here: 760 us
  waiting for transfers between devices  452 us (59%)
  other arithmetic  138 us (18%)
  blocking collectives  64.9 us (9%)
  matrix products  51.4 us (7%)
  local copies, waits for them, and re-layouts  30.6 us (4%)
  between operations  13.9 us (2%)
  starting transfers between devices  8.64 us (1%)
    scatter-add x16, other arithmetic, column_step(): return running.at[targets].add(matmul_result)  122 us
    reduce_scatter x1, waiting for transfers between devices, per_device(): lax.psum_scatter(partial_value.astype(jnp.bfloat16), 'rep', scatter_dimen...  101 us
    all_gather x1, waiting for transfers between devices, per_device(): shard_rows = lax.all_gather(projected, 'blk', axis=0, tiled=True)  89 us
    reduce_scatter x1, waiting for transfers between devices, per_device(): lax.psum_scatter(column_contribution.reshape(column_indices * tile_size,...  88.7 us
    psum x1, waiting for transfers between devices, per_device(): weight_sum, bias_sum = lax.psum((local_weight, local_bias), ('blk', 'rep'))  83.4 us
    all_gather x1, waiting for transfers between devices, per_device(): pre_grad = lax.all_gather(own_grad, 'rep', axis=0, tiled=True)  73.5 us
    psum x1, blocking collectives, per_device(): weight_sum, bias_sum = lax.psum((local_weight, local_bias), ('blk', 'rep'))  64.9 us
    dot_general x16, matrix products, column_step(): jnp.einsum('jab,bf->jaf', adjacency_tile, inputs, preferred_element_type=...  28 us
  transfers between devices with their start and end apart: 6, of which 6 were waited for; matrix products, arithmetic and copies ran while one was open for 1% of the time, Pallas kernels for 0%

commit v1 on v0

--- a/solution.py
+++ b/solution.py
@@ -39,7 +39,9 @@
     ]
     projected = jnp.dot(features, weight, preferred_element_type=jnp.float32).astype(jnp.bfloat16)
     zero_rows = jnp.zeros((row_tiles, tile_size, feature_width), jnp.float32)
-    shard_rows = lax.all_gather(projected, "blk", axis=0, tiled=True)
+    shard_rows = jnp.concatenate(
+        lax.all_to_all(jnp.stack([projected] * lax.axis_size("blk")), "blk", 0, 0), axis=0
+    )
 
     def column_step(step_index, running):
         adjacency_tile = lax.dynamic_index_in_dim(tile_stack, step_index, 0, keepdims=False)

time: 762 us -> 727 us (0.954)
  waiting for transfers between devices: 452 us -> 409 us
    all_gather x1 -> x0, waiting for transfers between devices: 89 us -> none  [per_device(): shard_rows = lax.all_gather(projected, 'blk', axis=0, tiled=True)]
    all_to_all x0 -> x1, waiting for transfers between devices: none -> 48.2 us  [per_device(): lax.all_to_all(jnp.stack([projected] * lax.axis_size('blk')), 'blk', 0, 0)]
where the time goes in v1:
time: 727 us; the launch traced here: 725 us
  waiting for transfers between devices  409 us (56%)
  other arithmetic  138 us (19%)
  blocking collectives  64.9 us (9%)
  matrix products  50.6 us (7%)
  local copies, waits for them, and re-layouts  33.7 us (5%)
  between operations  13.9 us (2%)
  starting transfers between devices  13.8 us (2%)
    scatter-add x16, other arithmetic, column_step(): return running.at[targets].add(matmul_result)  122 us
    reduce_scatter x1, waiting for transfers between devices, per_device(): lax.psum_scatter(partial_value.astype(jnp.bfloat16), 'rep', scatter_dimen...  99.3 us
    reduce_scatter x1, waiting for transfers between devices, per_device(): lax.psum_scatter(column_contribution.reshape(column_indices * tile_size,...  88.7 us
    psum x1, waiting for transfers between devices, per_device(): weight_sum, bias_sum = lax.psum((local_weight, local_bias), ('blk', 'rep'))  83.5 us
    all_gather x1, waiting for transfers between devices, per_device(): pre_grad = lax.all_gather(own_grad, 'rep', axis=0, tiled=True)  73.5 us
    psum x1, blocking collectives, per_device(): weight_sum, bias_sum = lax.psum((local_weight, local_bias), ('blk', 'rep'))  64.9 us
    all_to_all x1, waiting for transfers between devices, per_device(): lax.all_to_all(jnp.stack([projected] * lax.axis_size('blk')), 'blk', 0, 0)  48.2 us
    dot_general x16, matrix products, column_step(): jnp.einsum('jab,bf->jaf', adjacency_tile, inputs, preferred_element_type=...  28 us
  transfers between devices with their start and end apart: 6, of which 6 were waited for; matrix products, arithmetic and copies ran while one was open for 1% of the time, Pallas kernels for 0%

profile of v1, /device:TPU:1, one launch (start us, length us, event | category | flops | bytes accessed | tf_op | source)
XLA Modules:
  0.0 724.7 jit_solution(4416835266004581956)
XLA Ops:
  9.1 5.1 gather_fusion
  14.2 8.6 %all-to-all-start = ((bf16[16,64,512]{2,1,0:T(8,128)(2,1)}), bf16[16,64,512]{2,1,0:T(8,128)(2,1)S(1)}, u32[]{:S(2)}, u32[]{:S(2)}) async-start(bf16[16,64,512]{2,1,0:T(8,128)(2,1)} %bitcast.6), calls=%async_computation | async-start | bytes 2097152 | tf_op jit(solution)/shard_map/all_to_all | solution.py:29
  24.0 15.8 %all-to-all-done = bf16[16,64,512]{2,1,0:T(8,128)(2,1)S(1)} async-done(((bf16[16,64,512]{2,1,0:T(8,128)(2,1)}), bf16[16,64,512]{2,1,0:T(8,128)(2,1)S(1)}, u32[]{:S(2)}, u32[]{:S(2)}) %all-to-all-start) | async-done | bytes 1048608 | tf_op jit(solution)/shard_map/all_to_all | solution.py:29
  39.8 2.0 gather_fusion.1
  43.1 2.3 stack.2
  45.3 5.1 all-to-all-start.1
  50.6 48.2 %all-to-all-done.1 = bf16[8,512,512]{2,1,0:T(8,128)(2,1)} async-done(((bf16[8,512,512]{2,1,0:T(8,128)(2,1)}), bf16[8,512,512]{2,1,0:T(8,128)(2,1)}, u32[]{:S(2)}, u32[]{:S(2)}) %all-to-all-start.1) | async-done | bytes 4194336 | tf_op jit(solution)/shard_map/all_to_all | solution.py:43
  98.8 7.9 %broadcast_in_dim.18 = f32[32,256,512]{2,1,0:T(8,128)} broadcast(f32[]{:T(128)} %constant.89.clone.1), dimensions={} | broadcast | bytes 16777220 | tf_op jit(solution)/shard_map/broadcast_in_dim | solution.py:41
  106.7 150.8 %while.13 = (s32[]{:T(128)}, f32[32,256,512]{2,1,0:T(8,128)}, s32[16,6]{1,0:T(8,128)S(1)}, bf16[16,6,256,256]{3,2,1,0:T(8,128)(2,1)}, bf16[4096,512]{1,0:T(8,128...) while((s32[]{:T(128)}, f32[32,256,512]{2,1,0:T(8,128)}, s32[16,6]{1,0:T(8,128)S(1)}, ...), condition=%wide.region_6.7_spmd, body=%wide.region_4.6_spmd.sunk | while | flops 403439648 | bytes 13632219 | solution.py:55
  106.7 1.8 fusion.25
  108.4 7.6 %scatter_fusion = f32[32,256,512]{2,1,0:T(8,128)} fusion(f32[32,256,512]{2,1,0:T(8,128)} %get-tuple-element.171, s32[6]{0:T(128)S(1)} %fusion.24, f32[6,256,512]{2,1,0:T(8,128)S(1)} %fusion.25), kind=kCustom, calls=%fused_computation.3.clone.1 | custom fusion | flops 786432 | bytes 9437208 | tf_op jit(solution)/shard_map/while/body/eval_jaxpr/scatter-add | solution.py:53
  116.1 1.7 fusion.25
  117.8 7.7 %scatter_fusion = f32[32,256,512]{2,1,0:T(8,128)} fusion(f32[32,256,512]{2,1,0:T(8,128)} %get-tuple-element.171, s32[6]{0:T(128)S(1)} %fusion.24, f32[6,256,512]{2,1,0:T(8,128)S(1)} %fusion.25), kind=kCustom, calls=%fused_computation.3.clone.1 | custom fusion | flops 786432 | bytes 9437208 | tf_op jit(solution)/shard_map/while/body/eval_jaxpr/scatter-add | solution.py:53
  125.6 1.8 fusion.25
  127.3 7.6 %scatter_fusion = f32[32,256,512]{2,1,0:T(8,128)} fusion(f32[32,256,512]{2,1,0:T(8,128)} %get-tuple-element.171, s32[6]{0:T(128)S(1)} %fusion.24, f32[6,256,512]{2,1,0:T(8,128)S(1)} %fusion.25), kind=kCustom, calls=%fused_computation.3.clone.1 | custom fusion | flops 786432 | bytes 9437208 | tf_op jit(solution)/shard_map/while/body/eval_jaxpr/scatter-add | solution.py:53
  135.0 1.8 fusion.25
  136.7 7.7 %scatter_fusion = f32[32,256,512]{2,1,0:T(8,128)} fusion(f32[32,256,512]{2,1,0:T(8,128)} %get-tuple-element.171, s32[6]{0:T(128)S(1)} %fusion.24, f32[6,256,512]{2,1,0:T(8,128)S(1)} %fusion.25), kind=kCustom, calls=%fused_computation.3.clone.1 | custom fusion | flops 786432 | bytes 9437208 | tf_op jit(solution)/shard_map/while/body/eval_jaxpr/scatter-add | solution.py:53
  144.4 1.8 fusion.25
  146.2 7.7 %scatter_fusion = f32[32,256,512]{2,1,0:T(8,128)} fusion(f32[32,256,512]{2,1,0:T(8,128)} %get-tuple-element.171, s32[6]{0:T(128)S(1)} %fusion.24, f32[6,256,512]{2,1,0:T(8,128)S(1)} %fusion.25), kind=kCustom, calls=%fused_computation.3.clone.1 | custom fusion | flops 786432 | bytes 9437208 | tf_op jit(solution)/shard_map/while/body/eval_jaxpr/scatter-add | solution.py:53
  153.9 1.8 fusion.25
  155.7 7.6 %scatter_fusion = f32[32,256,512]{2,1,0:T(8,128)} fusion(f32[32,256,512]{2,1,0:T(8,128)} %get-tuple-element.171, s32[6]{0:T(128)S(1)} %fusion.24, f32[6,256,512]{2,1,0:T(8,128)S(1)} %fusion.25), kind=kCustom, calls=%fused_computation.3.clone.1 | custom fusion | flops 786432 | bytes 9437208 | tf_op jit(solution)/shard_map/while/body/eval_jaxpr/scatter-add | solution.py:53
  165.0 7.7 %scatter_fusion = f32[32,256,512]{2,1,0:T(8,128)} fusion(f32[32,256,512]{2,1,0:T(8,128)} %get-tuple-element.171, s32[6]{0:T(128)S(1)} %fusion.24, f32[6,256,512]{2,1,0:T(8,128)S(1)} %fusion.25), kind=kCustom, calls=%fused_computation.3.clone.1 | custom fusion | flops 786432 | bytes 9437208 | tf_op jit(solution)/shard_map/while/body/eval_jaxpr/scatter-add | solution.py:53
  174.5 7.6 %scatter_fusion = f32[32,256,512]{2,1,0:T(8,128)} fusion(f32[32,256,512]{2,1,0:T(8,128)} %get-tuple-element.171, s32[6]{0:T(128)S(1)} %fusion.24, f32[6,256,512]{2,1,0:T(8,128)S(1)} %fusion.25), kind=kCustom, calls=%fused_computation.3.clone.1 | custom fusion | flops 786432 | bytes 9437208 | tf_op jit(solution)/shard_map/while/body/eval_jaxpr/scatter-add | solution.py:53
  182.1 1.7 fusion.25
  183.9 7.6 %scatter_fusion = f32[32,256,512]{2,1,0:T(8,128)} fusion(f32[32,256,512]{2,1,0:T(8,128)} %get-tuple-element.171, s32[6]{0:T(128)S(1)} %fusion.24, f32[6,256,512]{2,1,0:T(8,128)S(1)} %fusion.25), kind=kCustom, calls=%fused_computation.3.clone.1 | custom fusion | flops 786432 | bytes 9437208 | tf_op jit(solution)/shard_map/while/body/eval_jaxpr/scatter-add | solution.py:53
  193.2 7.6 %scatter_fusion = f32[32,256,512]{2,1,0:T(8,128)} fusion(f32[32,256,512]{2,1,0:T(8,128)} %get-tuple-element.171, s32[6]{0:T(128)S(1)} %fusion.24, f32[6,256,512]{2,1,0:T(8,128)S(1)} %fusion.25), kind=kCustom, calls=%fused_computation.3.clone.1 | custom fusion | flops 786432 | bytes 9437208 | tf_op jit(solution)/shard_map/while/body/eval_jaxpr/scatter-add | solution.py:53
  200.9 1.8 fusion.25
  202.7 7.7 %scatter_fusion = f32[32,256,512]{2,1,0:T(8,128)} fusion(f32[32,256,512]{2,1,0:T(8,128)} %get-tuple-element.171, s32[6]{0:T(128)S(1)} %fusion.24, f32[6,256,512]{2,1,0:T(8,128)S(1)} %fusion.25), kind=kCustom, calls=%fused_computation.3.clone.1 | custom fusion | flops 786432 | bytes 9437208 | tf_op jit(solution)/shard_map/while/body/eval_jaxpr/scatter-add | solution.py:53
  212.1 7.6 %scatter_fusion = f32[32,256,512]{2,1,0:T(8,128)} fusion(f32[32,256,512]{2,1,0:T(8,128)} %get-tuple-element.171, s32[6]{0:T(128)S(1)} %fusion.24, f32[6,256,512]{2,1,0:T(8,128)S(1)} %fusion.25), kind=kCustom, calls=%fused_computation.3.clone.1 | custom fusion | flops 786432 | bytes 9437208 | tf_op jit(solution)/shard_map/while/body/eval_jaxpr/scatter-add | solution.py:53
  219.8 1.8 fusion.25
  221.6 7.7 %scatter_fusion = f32[32,256,512]{2,1,0:T(8,128)} fusion(f32[32,256,512]{2,1,0:T(8,128)} %get-tuple-element.171, s32[6]{0:T(128)S(1)} %fusion.24, f32[6,256,512]{2,1,0:T(8,128)S(1)} %fusion.25), kind=kCustom, calls=%fused_computation.3.clone.1 | custom fusion | flops 786432 | bytes 9437208 | tf_op jit(solution)/shard_map/while/body/eval_jaxpr/scatter-add | solution.py:53
  231.0 7.6 %scatter_fusion = f32[32,256,512]{2,1,0:T(8,128)} fusion(f32[32,256,512]{2,1,0:T(8,128)} %get-tuple-element.171, s32[6]{0:T(128)S(1)} %fusion.24, f32[6,256,512]{2,1,0:T(8,128)S(1)} %fusion.25), kind=kCustom, calls=%fused_computation.3.clone.1 | custom fusion | flops 786432 | bytes 9437208 | tf_op jit(solution)/shard_map/while/body/eval_jaxpr/scatter-add | solution.py:53
  238.7 1.7 fusion.25
  240.4 7.6 %scatter_fusion = f32[32,256,512]{2,1,0:T(8,128)} fusion(f32[32,256,512]{2,1,0:T(8,128)} %get-tuple-element.171, s32[6]{0:T(128)S(1)} %fusion.24, f32[6,256,512]{2,1,0:T(8,128)S(1)} %fusion.25), kind=kCustom, calls=%fused_computation.3.clone.1 | custom fusion | flops 786432 | bytes 9437208 | tf_op jit(solution)/shard_map/while/body/eval_jaxpr/scatter-add | solution.py:53
  248.1 1.8 fusion.25
  249.8 7.6 %scatter_fusion = f32[32,256,512]{2,1,0:T(8,128)} fusion(f32[32,256,512]{2,1,0:T(8,128)} %get-tuple-element.171, s32[6]{0:T(128)S(1)} %fusion.24, f32[6,256,512]{2,1,0:T(8,128)S(1)} %fusion.25), kind=kCustom, calls=%fused_computation.3.clone.1 | custom fusion | flops 786432 | bytes 9437208 | tf_op jit(solution)/shard_map/while/body/eval_jaxpr/scatter-add | solution.py:53
  257.5 9.1 %convert_element_type.41 = bf16[32,256,512]{2,1,0:T(8,128)(2,1)} convert(f32[32,256,512]{2,1,0:T(8,128)} %get-tuple-element.99) | non-fusion elementwise | flops 4194304 | bytes 25165824 | tf_op jit(solution)/shard_map/convert_element_type | solution.py:59
  266.7 99.3 %reduce-scatter.3.cloned.1.call-done = bf16[512,512]{1,0:T(8,128)(2,1)} async-done(((bf16[8192,512]{1,0:T(8,128)(2,1)}), bf16[512,512]{1,0:T(8,128)(2,1)}) %reduce-scatter.3.cloned.1.call-update) | async-done | bytes 524304 | tf_op jit(solution)/shard_map/reduce_scatter | solution.py:58
  366.0 2.5 convert_reduce_fusion
  368.8 73.5 %all-gather.2.cloned.1.call-done = bf16[8192,512]{1,0:T(8,128)(2,1)} async-done(((bf16[512,512]{1,0:T(8,128)(2,1)}), bf16[8192,512]{1,0:T(8,128)(2,1)}) %all-gather.2.cloned.1.call-update) | async-done | bytes 8388624 | tf_op jit(solution)/shard_map/all_gather | solution.py:64
  442.3 13.6 %gather_fusion.2 = bf16[96,256,512]{2,1,0:T(8,128)(2,1)} fusion(bf16[32,256,512]{2,1,0:T(8,128)(2,1)} %bitcast.60, s32[1024]{0:T(1024)S(1)} %pad_clamp_fusion), kind=kCustom, calls=%fused_computation.2 | custom fusion | bytes 50332032 | tf_op jit(solution)/shard_map/gather | solution.py:70
  455.9 17.4 %bitcast_convert_fusion = bf16[16,512,256]{1,2,0:T(8,128)(2,1)} fusion(bf16[16,6,256,512]{3,2,1,0:T(8,128)(2,1)} %bitcast.63, bf16[1,1,16,6,256,256]{5,4,3,2,1,0:T(8,128)(2,1)} %bitcast.66), kind=kOutput, calls=%fused_computation.14 | convolution fusion | flops 6444548096 | bytes 41943040 | tf_op jit(solution)/shard_map/nzqm,nzqg->nmg/dot_general | solution.py:71
  473.4 88.7 %reduce-scatter.5.cloned.1.call-done = bf16[512,512]{1,0:T(8,128)(2,1)} async-done(((bf16[4096,512]{1,0:T(8,128)(2,1)}), bf16[512,512]{1,0:T(8,128)(2,1)}) %reduce-scatter.5.cloned.1.call-update) | async-done | bytes 524304 | tf_op jit(solution)/shard_map/reduce_scatter | solution.py:74
  562.1 2.5 fusion.10
  564.6 64.9 %psum.15 = f32[512]{0:T(512)S(1)} all-reduce(f32[512]{0:T(512)S(1)} %get-tuple-element.125), channel_id=1, replica_groups=mesh['blk'=8,'rep'=16] {'blk','rep'}, use_global_device_ids=true, to_apply=%region_11.12 | all-reduce | flops 512 | bytes 4096 | tf_op jit(solution)/shard_map/psum | solution.py:82
  630.0 2.3 convolution_convert_fusion
  632.3 83.5 %all-reduce.2.cloned.1.call-done = f32[512,512]{1,0:T(8,128)} async-done(((f32[512,512]{1,0:T(8,128)}), f32[512,512]{1,0:T(8,128)}) %all-reduce.2.cloned.1.call-update) | async-done | bytes 1048592 | tf_op jit(solution)/shard_map/psum | solution.py:82
  715.8 2.3 broadcast_multiply_fusion
  (73 shorter events, 14.4 us)
Async XLA Ops:
  7.2 1.9 copy-start
  7.2 34.6 %copy-start.4 = (bf16[512,512]{1,0:T(8,128)(2,1)S(1)}, bf16[512,512]{1,0:T(8,128)(2,1)}, u32[]{:S(2)}) copy-start(bf16[512,512]{1,0:T(8,128)(2,1)} %param.11) | copy-start | bytes 1572868
  14.2 36.3 %copy-start.8 = (s32[1,1,16,6]{2,1,3,0:T(1,128)S(1)}, s32[1,1,16,6]{2,1,3,0:T(1,128)}, u32[]{:S(2)}) copy-start(s32[1,1,16,6]{2,1,3,0:T(1,128)} %param.13) | copy-start | bytes 1156
  14.2 25.6 %all-to-all-start = ((bf16[16,64,512]{2,1,0:T(8,128)(2,1)}), bf16[16,64,512]{2,1,0:T(8,128)(2,1)S(1)}, u32[]{:S(2)}, u32[]{:S(2)}) async-start(bf16[16,64,512]{2,1,0:T(8,128)(2,1)} %bitcast.6), calls=%async_computation | async-start | bytes 2097152 | tf_op jit(solution)/shard_map/all_to_all | solution.py:29
  41.8 64.9 %copy-start.2 = (bf16[512,512]{1,0:T(8,128)(2,1)}, bf16[512,512]{1,0:T(8,128)(2,1)S(1)}, u32[]{:S(2)}) copy-start(bf16[512,512]{1,0:T(8,128)(2,1)S(1)} %gather_fusion.1) | copy-start | bytes 1572868
  42.3 0.8 copy-start.6
  45.3 53.4 %all-to-all-start.1 = ((bf16[8,512,512]{2,1,0:T(8,128)(2,1)}), bf16[8,512,512]{2,1,0:T(8,128)(2,1)}, u32[]{:S(2)}, u32[]{:S(2)}) async-start(bf16[8,512,512]{2,1,0:T(8,128)(2,1)} %stack.2), calls=%async_computation.1 | async-start | bytes 8388608 | tf_op jit(solution)/shard_map/all_to_all | solution.py:43
  50.4 315.5 %reduce-scatter.3.cloned.1.call-start = ((), (), s32[]{:S(2)}) async-start(), calls=%async_computation.4 | async-start | bytes 8912896 | tf_op jit(solution)/shard_map/reduce_scatter | solution.py:58
  257.5 108.5 %copy-start.7 = (bf16[512,512]{1,0:T(8,128)(2,1)S(1)}, bf16[512,512]{1,0:T(8,128)(2,1)}, u32[]{:S(2)}) copy-start(bf16[512,512]{1,0:T(8,128)(2,1)} %param.15) | copy-start | bytes 1572868
  257.5 108.5 %copy-start.9 = (f32[512]{0:T(512)S(1)}, f32[512]{0:T(512)}, u32[]{:S(2)}) copy-start(f32[512]{0:T(512)} %param.12) | copy-start | bytes 6148
  266.6 175.7 %all-gather.2.cloned.1.call-start = ((), (), s32[]{:S(2)}) async-start(), calls=%async_computation.5 | async-start | bytes 8912896 | tf_op jit(solution)/shard_map/all_gather | solution.py:64
  368.5 193.5 %reduce-scatter.5.cloned.1.call-start = ((), (), s32[]{:S(2)}) async-start(), calls=%async_computation.6 | async-start | bytes 4718592 | tf_op jit(solution)/shard_map/reduce_scatter | solution.py:74
  455.9 106.2 %copy-start.3 = (bf16[512,512]{1,0:T(8,128)(2,1)S(1)}, bf16[512,512]{1,0:T(8,128)(2,1)}, u32[]{:S(2)}) copy-start(bf16[512,512]{1,0:T(8,128)(2,1)} %copy-done.2) | copy-start | bytes 1572868
  455.9 174.1 %copy-start.5 = (bf16[512,512]{1,0:T(8,128)(2,1)S(1)}, bf16[512,512]{1,0:T(8,128)(2,1)}, u32[]{:S(2)}) copy-start(bf16[512,512]{1,0:T(8,128)(2,1)} %param.11) | copy-start | bytes 1572868
  455.9 262.2 %copy-start.1 = (bf16[1024,512]{1,0:T(8,128)(2,1)S(1)}, bf16[1024,512]{1,0:T(8,128)(2,1)}, u32[]{:S(2)}) copy-start(bf16[1024,512]{1,0:T(8,128)(2,1)} %param.9) | copy-start | bytes 3145732
  473.3 242.5 %all-reduce.2.cloned.1.call-start = ((), (), s32[]{:S(2)}) async-start(), calls=%async_computation.7 | async-start | bytes 2097152 | tf_op jit(solution)/shard_map/psum | solution.py:82
Sparse Core Ops, SparseCore 0:
  266.8 99.1 reduce-scatter.2
  369.0 73.2 all-gather.1
  473.4 88.5 reduce-scatter.4
  567.3 148.4 all-reduce.1
